TPU v7x, 128 devices: a whole 4x4x4 slice. The times are simulated.
128 devices in a mesh: tok: 16 (over y, x), head: 8 (over z, core).
Axes of the slice: x: 4, y: 4, z: 4, core: 2. Of those that a mesh axis runs over, the one named last changes fastest.
Arguments:
- tokens: bfloat16 [8192, 8192], P('tok', 'head'), may hold values from -60 to 60
- gain: bfloat16 [8192], P('head'), may hold values from 0.5 to 2
- w_query: bfloat16 [8192, 8, 512], P(('head', 'tok')), may hold values from -0.125 to 0.125
- w_key: bfloat16 [8192, 8, 128], P(('head', 'tok')), may hold values from -0.0625 to 0.0625
- w_value: bfloat16 [8192, 8, 128], P(('head', 'tok')), may hold values from -0.5 to 0.5
- group_ids: int32 [8192, 1], P('tok'), may hold values from 0 to 15; in each aligned block of 512 rows (0 to 511, 512 to 1023, ...) at most 64 rows name the same one
- key_pages: bfloat16 [1024, 128, 8, 128], P('tok', None, 'head'), may hold values from -42 to 42
- value_pages: bfloat16 [1024, 128, 8, 128], P('tok', None, 'head'), may hold values from -48 to 48
- page_table: int32 [16, 32], P('tok'), may hold values from 0 to 1023, as said below
Outputs:
- attention: bfloat16 [8192, 4096], P('tok', 'head')
Inputs may be any that keep to these rules, and one draw needn't show every extreme that they name: `group_ids`: among the 512 tokens of one index of tok (aligned blocks of rows), no group appears more than 64 times, a bound that some block reaches. `page_table`: row g lists 32 different pages, all in g * 64 to (g + 1) * 64 - 1, among them the first and the last page of that range.
All inputs are finite; a program needn't handle non-finite values.
Results may differ from a plain program's by a relative error of at most 0.0085.
The roundings to bfloat16 on the way count: a program that leaves them out, or rounds other values in their place, can miss the bound.
Values may be sent and summed in bfloat16 or wider, within the bound.
No kernel may reach another device: no remote copies, remote signals or barrier semaphores. Data moves between devices by JAX's collectives and lax.ppermute only.
A program may use at most 128 MiB of HBM per device.

v0:
```python
import math
import jax
import jax.numpy as jnp
from jax import lax
from jax.sharding import PartitionSpec as P

EPS = 1e-05
THETA = 10000.0


def rotate(values, positions):
    halfway = values.shape[-1] // 2
    frequency = jnp.exp(
        -math.log(THETA) * 2.0 * jnp.arange(halfway, dtype=jnp.float32) / values.shape[-1]
    )
    angles = positions.astype(jnp.float32)[:, None] * frequency[None, :]
    cosine = jnp.cos(angles)[:, None, :]
    sine_part = jnp.sin(angles)[:, None, :]
    leading = values[..., :halfway].astype(jnp.float32)
    trailing = values[..., halfway:].astype(jnp.float32)
    return jnp.concatenate(
        [leading * cosine - trailing * sine_part, trailing * cosine + leading * sine_part], axis=-1
    ).astype(jnp.bfloat16)


def attend(
    queries, query_rank, prefix_keys, prefix_values, new_keys, new_values, key_rank, key_live
):
    scaling = 1.0 / math.sqrt(queries.shape[-1])
    before = (
        jnp.einsum("bhd,pd->bhp", queries, prefix_keys, preferred_element_type=jnp.float32)
        * scaling
    )
    inside = (
        jnp.einsum("bhd,sd->bhs", queries, new_keys, preferred_element_type=jnp.float32) * scaling
    )
    allowed = key_live[None, :] & (key_rank[None, :] <= query_rank[:, None])
    inside = jnp.where(allowed[:, None, :], inside, -jnp.inf)
    highest = jnp.maximum(jnp.max(before, axis=-1), jnp.max(inside, axis=-1))
    expo_before = jnp.exp(before - highest[..., None])
    expo_inside = jnp.exp(inside - highest[..., None])
    totals = jnp.sum(expo_before, axis=-1) + jnp.sum(expo_inside, axis=-1)
    mixed = jnp.einsum(
        "bhp,pd->bhd",
        expo_before.astype(jnp.bfloat16),
        prefix_values,
        preferred_element_type=jnp.float32,
    )
    mixed = mixed + jnp.einsum(
        "bhs,sd->bhd",
        expo_inside.astype(jnp.bfloat16),
        new_values,
        preferred_element_type=jnp.float32,
    )
    return (mixed / totals[..., None]).astype(jnp.bfloat16)


def row_norm(tokens, gain, full_width):
    values_wide = tokens.astype(jnp.float32)
    squares = lax.psum(jnp.sum(values_wide * values_wide, axis=1), "head")
    factor = lax.rsqrt(squares / full_width + EPS)
    return (values_wide * factor[:, None] * gain.astype(jnp.float32)[None, :]).astype(jnp.bfloat16)


def body(tokens, gain, w_query, w_key, w_value, group_ids, key_pages, value_pages, page_table):
    row_count = tokens.shape[0]
    n_tok = lax.axis_size("tok")
    n_head = lax.axis_size("head")
    head_size = key_pages.shape[-1]
    query_width = w_query.shape[2]
    group_heads = query_width // head_size
    full_width = tokens.shape[1] * n_head
    capacity = 2 * row_count // n_tok
    normed = row_norm(tokens, gain, full_width)
    gathered = (
        lax.all_gather(w_query, "tok", axis=0, tiled=True),
        lax.all_gather(w_key, "tok", axis=0, tiled=True),
        lax.all_gather(w_value, "tok", axis=0, tiled=True),
    )
    group_count = row_count * lax.axis_size("head") // row_count
    results = []
    for weight in gathered:
        results.append(
            jnp.einsum("rd,dnc->nrc", normed, weight, preferred_element_type=jnp.float32)
        )
    joined = jnp.concatenate(results, axis=2)
    projected = lax.psum_scatter(
        joined.reshape(group_count * row_count, joined.shape[2]),
        "head",
        scatter_dimension=0,
        tiled=True,
    )
    projected_low = projected.astype(jnp.bfloat16)
    width_all = projected_low.shape[1]
    group_of = group_ids[:, 0]
    member = (group_of[:, None] == jnp.arange(n_tok, dtype=jnp.int32)[None, :]).astype(jnp.int32)
    local_rank = jnp.sum((jnp.cumsum(member, axis=0) - member) * member, axis=1)
    slot_index = group_of * capacity + local_rank
    outgoing = (
        jnp.zeros((n_tok * capacity, width_all), jnp.bfloat16).at[slot_index].set(projected_low)
    )
    marker = jnp.zeros((n_tok * capacity,), jnp.bfloat16).at[slot_index].set(1.0)
    arrived, arrived_marker = (
        lax.all_to_all(
            outgoing.reshape(n_tok, capacity, width_all),
            "tok",
            split_axis=0,
            concat_axis=0,
            tiled=True,
        ),
        lax.all_to_all(
            marker.reshape(n_tok, capacity), "tok", split_axis=0, concat_axis=0, tiled=True
        ),
    )
    slot_total = n_tok * capacity
    arrived = arrived.reshape(slot_total, width_all)
    live_count = (arrived_marker.reshape(slot_total) > 0).astype(jnp.int32)
    key_live = live_count > 0
    slot_rank = jnp.cumsum(live_count) - live_count
    prefix_length = page_table.shape[1] * key_pages.shape[1]
    positions = prefix_length + slot_rank
    rotated_queries = rotate(
        arrived[:, :query_width].reshape(slot_total, group_heads, head_size), positions
    )
    rotated_keys = rotate(
        arrived[:, query_width : query_width + head_size].reshape(slot_total, 1, head_size),
        positions,
    )[:, 0, :]
    slot_values = arrived[:, query_width + head_size :]
    local_pages = page_table[0] - lax.axis_index("tok") * key_pages.shape[0]
    prefix_keys = jnp.take(key_pages[:, :, 0, :], local_pages, axis=0).reshape(
        prefix_length, head_size
    )
    prefix_values = jnp.take(value_pages[:, :, 0, :], local_pages, axis=0).reshape(
        prefix_length, head_size
    )
    block_size = min(128, slot_total)

    def one_block(blocked):
        return attend(
            blocked[0],
            blocked[1],
            prefix_keys,
            prefix_values,
            rotated_keys,
            slot_values,
            slot_rank,
            key_live,
        )

    attended = lax.map(
        one_block,
        (
            rotated_queries.reshape(slot_total // block_size, block_size, group_heads, head_size),
            slot_rank.reshape(slot_total // block_size, block_size),
        ),
    )
    returned = lax.all_to_all(
        attended.reshape(n_tok, capacity, query_width),
        "tok",
        split_axis=0,
        concat_axis=0,
        tiled=True,
    )
    return returned.reshape(n_tok * capacity, query_width)[slot_index]


def solution(mesh):
    placed = (
        P("tok", "head"),
        P("head"),
        P(("head", "tok"), None, None),
        P(("head", "tok"), None, None),
        P(("head", "tok"), None, None),
        P("tok", None),
        P("tok", None, "head", None),
        P("tok", None, "head", None),
        P("tok", None),
    )
    return jax.shard_map(
        body, mesh=mesh, in_specs=placed, out_specs=P("tok", "head"), check_vma=False
    )
```

profile of v0, /device:TPU:32, one launch (start us, length us, event | category | flops | bytes accessed | tf_op | source)
XLA Modules:
  0.0 415.2 jit_solution(10881437984728749985)
XLA Ops:
  6.5 1.7 copy.34
  8.3 1.6 copy.33
  10.0 2.0 copy.32
  12.4 12.5 %psum.7 = f32[512]{0:T(512)S(1)} all-reduce(f32[512]{0:T(512)S(1)} %fusion.30), channel_id=1, replica_groups=mesh['tok'=16,'head'=8] {'head'}, use_global_device_ids=true, to_apply=%region_4.5 | all-reduce | flops 512 | bytes 4096 | tf_op jit(solution)/shard_map/psum | solution.py:60
  24.9 31.4 %all-gather.8.cloned.1.call-done = bf16[1024,8,128]{2,0,1:T(8,128)(2,1)} async-done(((bf16[64,8,128]{2,0,1:T(8,128)(2,1)}), bf16[1024,8,128]{2,0,1:T(8,128)(2,1)}) %all-gather.8.cloned.1.call-update) | async-done | bytes 2097168 | tf_op jit(solution)/shard_map/all_gather | solution.py:78
  56.3 4.3 %convolution_bitcast_fusion.1 = f32[8,512,128]{1,2,0:T(8,128)} fusion(bf16[1024,8,128]{2,0,1:T(8,128)(2,1)} %all-gather.8.cloned.1.call-done, bf16[512,1024]{1,0:T(8,128)(2,1)S(1)} %copy-done.4, f32[1024]{0:T(1024)S(1)} %convert_element_type.74, f32[512]{0:T(512)S(1)} %add_rsqrt_fusion), kind=kOutput, calls=%fused_computation.48 | convolution fusion | flops 1075838976 | bytes 5249024 | tf_op jit(solution)/shard_map/rd,dnc->nrc/dot_general | solution.py:84
  60.6 42.0 %all-gather.6.cloned.1.call-done = bf16[1024,8,128]{2,0,1:T(8,128)(2,1)} async-done(((bf16[64,8,128]{2,0,1:T(8,128)(2,1)}), bf16[1024,8,128]{2,0,1:T(8,128)(2,1)}) %all-gather.6.cloned.1.call-update) | async-done | bytes 2097168 | tf_op jit(solution)/shard_map/all_gather | solution.py:77
  102.6 4.3 %convolution_bitcast_fusion.2 = f32[8,512,128]{1,2,0:T(8,128)} fusion(bf16[1024,8,128]{2,0,1:T(8,128)(2,1)} %all-gather.6.cloned.1.call-done, bf16[512,1024]{1,0:T(8,128)(2,1)S(1)} %copy-done.4, f32[1024]{0:T(1024)S(1)} %convert_element_type.74, f32[512]{0:T(512)S(1)} %add_rsqrt_fusion), kind=kOutput, calls=%fused_computation.49 | convolution fusion | flops 1075838976 | bytes 5249024 | tf_op jit(solution)/shard_map/rd,dnc->nrc/dot_general | solution.py:84
  106.9 68.0 %all-gather.4.cloned.1.call-done = bf16[1024,8,512]{2,0,1:T(8,128)(2,1)} async-done(((bf16[64,8,512]{2,0,1:T(8,128)(2,1)}), bf16[1024,8,512]{2,0,1:T(8,128)(2,1)}) %all-gather.4.cloned.1.call-update) | async-done | bytes 8388624 | tf_op jit(solution)/shard_map/all_gather | solution.py:76
  174.9 7.5 %convolution_bitcast_fusion = f32[8,512,512]{1,2,0:T(8,128)S(1)} fusion(bf16[1024,8,512]{2,0,1:T(8,128)(2,1)} %all-gather.4.cloned.1.call-done, bf16[512,1024]{1,0:T(8,128)(2,1)S(1)} %copy-done.4, f32[1024]{0:T(1024)S(1)} %convert_element_type.74, f32[512]{0:T(512)S(1)} %add_rsqrt_fusion), kind=kOutput, calls=%fused_computation.42 | convolution fusion | flops 4297064448 | bytes 17831936 | tf_op jit(solution)/shard_map/rd,dnc->nrc/dot_general | solution.py:84
  182.4 6.9 %pad_maximum_fusion = f32[8,512,768]{1,2,0:T(8,128)} fusion(f32[8,512,128]{1,2,0:T(8,128)S(1)} %copy-done.2, f32[8,512,128]{1,2,0:T(8,128)S(1)} %copy-done.3, f32[8,512,512]{1,2,0:T(8,128)S(1)} %convolution_bitcast_fusion), kind=kLoop, calls=%fused_computation.41 | loop fusion | flops 6291456 | bytes 25165824 | tf_op jit(solution)/shard_map/concatenate | solution.py:86
  189.3 12.6 %copy.35 = f32[8,512,768]{2,1,0:T(8,128)} copy(f32[8,512,768]{1,2,0:T(8,128)} %pad_maximum_fusion) | data formatting | bytes 25165824 | tf_op jit(solution)/shard_map/concatenate | solution.py:86
  204.1 3.8 scatter_custom_fusion.1
  208.5 5.3 %all-to-all-start.1 = ((bf16[16,1,64]{2,1,0:T(2,128)(2,1)}), bf16[16,1,64]{2,1,0:T(2,128)(2,1)S(1)}, u32[]{:S(2)}, u32[]{:S(2)}) async-start(bf16[16,1,64]{2,1,0:T(2,128)(2,1)} %all_to_all.16), calls=%async_computation.2 | async-start | bytes 16384 | tf_op jit(solution)/shard_map/all_to_all | solution.py:111
  214.6 3.3 gather_fusion.2
  217.9 53.8 %reduce-scatter.2.cloned.1.call-done = f32[512,768]{1,0:T(8,128)} async-done(((f32[4096,768]{1,0:T(8,128)}), f32[512,768]{1,0:T(8,128)}) %reduce-scatter.2.cloned.1.call-update) | async-done | bytes 1572880 | tf_op jit(solution)/shard_map/reduce_scatter | solution.py:87
  271.7 4.6 %scatter_custom_fusion = bf16[1024,768]{1,0:T(8,128)(2,1)} fusion(s32[512]{0:T(512)S(1)} %bitcast.131, f32[512,768]{1,0:T(8,128)} %reduce-scatter.2.cloned.1.call-done, bf16[]{:T(256)} %constant.23.clone.1), kind=kCustom, calls=%fused_computation.62 | custom fusion | flops 393216 | bytes 3145730 | tf_op jit(solution)/shard_map/scatter | solution.py:100
  276.3 7.1 %all-to-all-start = ((bf16[16,64,768]{2,1,0:T(8,128)(2,1)}), bf16[16,64,768]{2,1,0:T(8,128)(2,1)}, u32[]{:S(2)}, u32[]{:S(2)}) async-start(bf16[16,64,768]{2,1,0:T(8,128)(2,1)} %bitcast.17), calls=%async_computation.1 | async-start | bytes 3145728 | tf_op jit(solution)/shard_map/all_to_all | solution.py:104
  283.4 1.5 broadcast_select_fusion
  285.8 1.7 multiply_cosine_fusion.1
  287.5 23.9 %all-to-all-done = bf16[16,64,768]{2,1,0:T(8,128)(2,1)} async-done(((bf16[16,64,768]{2,1,0:T(8,128)(2,1)}), bf16[16,64,768]{2,1,0:T(8,128)(2,1)}, u32[]{:S(2)}, u32[]{:S(2)}) %all-to-all-start) | async-done | bytes 1572896 | tf_op jit(solution)/shard_map/all_to_all | solution.py:104
  311.4 1.8 fusion.61
  314.5 3.1 fusion.50
  318.9 1.6 fusion.34
  321.8 1.7 copy.39
  324.8 57.1 %while.10 = (s32[]{:T(128)}, bf16[8,128,4,128]{3,2,1,0:T(4,128)(2,1)}, bf16[8,128,4,128]{3,1,2,0:T(8,128)(2,1)S(1)}, bf16[4096,128]{1,0:T(8,128)(2,1)S(1)}, pred...) while((s32[]{:T(128)}, ...), condition=%wide.region_15.17_spmd, body=%wide.region_10.16_spmd.sunk | while | flops 1365179392 | bytes 36869268 | solution.py:151
  327.5 1.5 fusion.82
  329.0 1.5 fusion.81
  334.6 1.5 fusion.82
  336.1 1.5 fusion.81
  339.8 1.3 multiply_reduce_fusion.2
  341.7 1.5 fusion.82
  343.2 1.5 fusion.81
  346.9 1.3 multiply_reduce_fusion.2
  348.9 1.5 fusion.82
  350.4 1.5 fusion.81
  356.0 1.5 fusion.82
  357.5 1.5 fusion.81
  363.1 1.5 fusion.82
  364.6 1.5 fusion.81
  370.2 1.5 fusion.82
  371.8 1.5 fusion.81
  377.4 1.5 fusion.82
  378.9 1.5 fusion.81
  381.8 2.3 reshape.278
  384.1 3.7 all-to-all-start.2
  387.8 18.2 %all-to-all-done.2 = bf16[16,64,512]{2,1,0:T(8,128)(2,1)S(1)} async-done(((bf16[16,64,512]{2,1,0:T(8,128)(2,1)}), bf16[16,64,512]{2,1,0:T(8,128)(2,1)S(1)}, u32[]{:S(2)}, u32[]{:S(2)}) %all-to-all-start.2) | async-done | bytes 1048608 | tf_op jit(solution)/shard_map/all_to_all | solution.py:158
  406.0 2.6 gather_fusion
  (146 shorter events, 40.2 us)
Async XLA Ops:
  6.5 207.3 %copy-start = (bf16[64,128,1,128]{3,1,2,0:T(8,128)(2,1)S(1)}, bf16[64,128,1,128]{3,1,2,0:T(8,128)(2,1)}, u32[]{:S(2)}) copy-start(bf16[64,128,1,128]{3,1,2,0:T(8,128)(2,1)} %param.19) | copy-start | bytes 6291460
  6.5 5.5 %copy-start.7 = (bf16[1024]{0:T(1024)(128)(2,1)S(1)}, bf16[1024]{0:T(1024)(128)(2,1)}, u32[]{:S(2)}) copy-start(bf16[1024]{0:T(1024)(128)(2,1)} %param.14) | copy-start | bytes 6148
  6.5 5.5 %copy-start.4 = (bf16[512,1024]{1,0:T(8,128)(2,1)S(1)}, bf16[512,1024]{1,0:T(8,128)(2,1)}, u32[]{:S(2)}) copy-start(bf16[512,1024]{1,0:T(8,128)(2,1)} %param.13) | copy-start | bytes 3145732
  6.5 49.7 %all-gather.8.cloned.1.call-start = ((), (), s32[]{:S(2)}) async-start(), calls=%async_computation.6 | async-start | bytes 2228224 | tf_op jit(solution)/shard_map/all_gather | solution.py:78
  8.3 94.3 %all-gather.6.cloned.1.call-start = ((), (), s32[]{:S(2)}) async-start(), calls=%async_computation.5 | async-start | bytes 2228224 | tf_op jit(solution)/shard_map/all_gather | solution.py:77
  9.9 164.9 %all-gather.4.cloned.1.call-start = ((), (), s32[]{:S(2)}) async-start(), calls=%async_computation.4 | async-start | bytes 8912896 | tf_op jit(solution)/shard_map/all_gather | solution.py:76
  12.0 259.7 %reduce-scatter.2.cloned.1.call-start = ((), (), s32[]{:S(2)}) async-start(), calls=%async_computation.7 | async-start | bytes 14155776 | tf_op jit(solution)/shard_map/reduce_scatter | solution.py:87
  174.9 7.5 %copy-start.2 = (f32[8,512,128]{1,2,0:T(8,128)S(1)}, f32[8,512,128]{1,2,0:T(8,128)}, u32[]{:S(2)}) copy-start(f32[8,512,128]{1,2,0:T(8,128)} %convolution_bitcast_fusion.1) | copy-start | bytes 6291460
  174.9 7.6 %copy-start.3 = (f32[8,512,128]{1,2,0:T(8,128)S(1)}, f32[8,512,128]{1,2,0:T(8,128)}, u32[]{:S(2)}) copy-start(f32[8,512,128]{1,2,0:T(8,128)} %convolution_bitcast_fusion.2) | copy-start | bytes 6291460
  201.8 0.7 copy-start.6
  201.8 11.9 %copy-start.8 = (s32[1,32]{1,0:T(1,128)S(1)}, s32[1,32]{1,0:T(1,128)}, u32[]{:S(2)}) copy-start(s32[1,32]{1,0:T(1,128)} %param.21) | copy-start | bytes 388
  208.5 67.8 %all-to-all-start.1 = ((bf16[16,1,64]{2,1,0:T(2,128)(2,1)}), bf16[16,1,64]{2,1,0:T(2,128)(2,1)S(1)}, u32[]{:S(2)}, u32[]{:S(2)}) async-start(bf16[16,1,64]{2,1,0:T(2,128)(2,1)} %all_to_all.16), calls=%async_computation.2 | async-start | bytes 16384 | tf_op jit(solution)/shard_map/all_to_all | solution.py:111
  276.3 35.1 %all-to-all-start = ((bf16[16,64,768]{2,1,0:T(8,128)(2,1)}), bf16[16,64,768]{2,1,0:T(8,128)(2,1)}, u32[]{:S(2)}, u32[]{:S(2)}) async-start(bf16[16,64,768]{2,1,0:T(8,128)(2,1)} %bitcast.17), calls=%async_computation.1 | async-start | bytes 3145728 | tf_op jit(solution)/shard_map/all_to_all | solution.py:104
  329.0 1.5 copy-start.5
  336.1 1.5 copy-start.5
  343.2 1.5 copy-start.5
  350.4 1.5 copy-start.5
  357.5 1.5 copy-start.5
  364.6 1.5 copy-start.5
  371.8 1.5 copy-start.5
  378.9 1.5 copy-start.5
  384.1 21.9 %all-to-all-start.2 = ((bf16[16,64,512]{2,1,0:T(8,128)(2,1)}), bf16[16,64,512]{2,1,0:T(8,128)(2,1)S(1)}, u32[]{:S(2)}, u32[]{:S(2)}) async-start(bf16[16,64,512]{2,1,0:T(8,128)(2,1)} %reshape.278), calls=%async_computation.3 | async-start | bytes 2097152 | tf_op jit(solution)/shard_map/all_to_all | solution.py:158
  406.0 2.6 copy-start.1
Sparse Core Ops, SparseCore 0:
  9.5 46.7 all-gather.7
  58.4 44.1 all-gather.5
  104.8 70.0 all-gather.3
  202.0 69.6 reduce-scatter.1
where the time goes:
time: 416 us; the launch traced here: 415 us
  waiting for transfers between devices  237 us (57%)
  matrix products  48.6 us (12%)
  local copies, waits for them, and re-layouts  44.9 us (11%)
  other arithmetic  42 us (10%)
  starting transfers between devices  16.1 us (4%)
  between operations  13.4 us (3%)
  blocking collectives  12.5 us (3%)
    all_gather x1, waiting for transfers between devices, body(): lax.all_gather(w_query, 'tok', axis=0, tiled=True)  68 us
    reduce_scatter x1, waiting for transfers between devices, body(): lax.psum_scatter(joined.reshape(group_count * row_count, joined.shape[2])...  53.8 us
    all_gather x1, waiting for transfers between devices, body(): lax.all_gather(w_key, 'tok', axis=0, tiled=True)  42 us
    all_gather x1, waiting for transfers between devices, body(): lax.all_gather(w_value, 'tok', axis=0, tiled=True)  31.4 us
    all_to_all x1, waiting for transfers between devices, body(): lax.all_to_all(outgoing.reshape(n_tok, capacity, width_all), 'tok', split...  23.9 us
    all_to_all x1, waiting for transfers between devices, body(): lax.all_to_all(attended.reshape(n_tok, capacity, query_width), 'tok', spl...  18.2 us
    reduce_sum x16, other arithmetic, attend(): totals = jnp.sum(expo_before, axis=-1) + jnp.sum(expo_inside, axis=-1)  16.8 us
    dot_general x3, matrix products, body(): jnp.einsum('rd,dnc->nrc', normed, weight, preferred_element_type=jnp.floa...  16.1 us
  transfers between devices with their start and end apart: 7, of which 6 were waited for; matrix products, arithmetic and copies ran while one was open for 7% of the time, Pallas kernels for 0%

commit v1 on v0

--- a/solution.py
+++ b/solution.py
@@ -75,7 +75,9 @@
     gathered = (
         lax.all_gather(w_query, "tok", axis=0, tiled=True),
         lax.all_gather(w_key, "tok", axis=0, tiled=True),
-        lax.all_gather(w_value, "tok", axis=0, tiled=True),
+        jnp.concatenate(
+            lax.all_to_all(jnp.stack([w_value] * lax.axis_size("tok")), "tok", 0, 0), axis=0
+        ),
     )
     group_count = row_count * lax.axis_size("head") // row_count
     results = []

time: 416 us -> 387 us (0.930)
  waiting for transfers between devices: 237 us -> 195 us
  starting transfers between devices: 16.1 us -> 23.3 us
  local copies, waits for them, and re-layouts: 44.9 us -> 50.1 us
    all_gather x1, waiting for transfers between devices: 42 us -> 10.6 us  [body(): lax.all_gather(w_key, 'tok', axis=0, tiled=True)]
    all_gather x1 -> x0, waiting for transfers between devices: 31.4 us -> none  [body(): lax.all_gather(w_value, 'tok', axis=0, tiled=True)]
    all_to_all x0 -> x1, waiting for transfers between devices: none -> 21 us  [body(): lax.all_to_all(jnp.stack([w_value] * lax.axis_size('tok')), 'tok', 0, 0)]
    all_to_all x0 -> x1, starting transfers between devices: none -> 7.22 us  [body(): lax.all_to_all(jnp.stack([w_value] * lax.axis_size('tok')), 'tok', 0, 0)]
    dot_general x3 -> x2, matrix products: 16.1 us -> 11.9 us  [body(): jnp.einsum('rd,dnc->nrc', normed, weight, preferred_element_type=jnp.floa...]
    unnamed x0 -> x1, matrix products: none -> 4.25 us
  transfers between devices with their start and end apart: 7 -> 7, of which waited for: 6 -> 6; matrix products, arithmetic and copies ran while one was open for 7% -> 9% of each run, Pallas kernels for 0% -> 0%
where the time goes in v1:
time: 387 us; the launch traced here: 386 us
  waiting for transfers between devices  195 us (50%)
  local copies, waits for them, and re-layouts  50.1 us (13%)
  matrix products  48.6 us (13%)
  other arithmetic  42 us (11%)
  starting transfers between devices  23.3 us (6%)
  between operations  13.4 us (3%)
  blocking collectives  12.6 us (3%)
    all_gather x1, waiting for transfers between devices, body(): lax.all_gather(w_query, 'tok', axis=0, tiled=True)  67.9 us
    reduce_scatter x1, waiting for transfers between devices, body(): lax.psum_scatter(joined.reshape(group_count * row_count, joined.shape[2])...  53.8 us
    all_to_all x1, waiting for transfers between devices, body(): lax.all_to_all(outgoing.reshape(n_tok, capacity, width_all), 'tok', split...  23.9 us
    all_to_all x1, waiting for transfers between devices, body(): lax.all_to_all(jnp.stack([w_value] * lax.axis_size('tok')), 'tok', 0, 0)  21 us
    all_to_all x1, waiting for transfers between devices, body(): lax.all_to_all(attended.reshape(n_tok, capacity, query_width), 'tok', spl...  18.2 us
    reduce_sum x16, other arithmetic, attend(): totals = jnp.sum(expo_before, axis=-1) + jnp.sum(expo_inside, axis=-1)  16.8 us
    psum x1, blocking collectives, row_norm(): squares = lax.psum(jnp.sum(values_wide * values_wide, axis=1), 'head')  12.6 us
    concatenate x1, local copies, waits for them, and re-layouts, body(): joined = jnp.concatenate(results, axis=2)  12.6 us
  transfers between devices with their start and end apart: 7, of which 6 were waited for; matrix products, arithmetic and copies ran while one was open for 9% of the time, Pallas kernels for 0%

profile of v1, /device:TPU:32, one launch (start us, length us, event | category | flops | bytes accessed | tf_op | source)
XLA Modules:
  0.0 385.8 jit_solution(7453260482781046610)
XLA Ops:
  6.5 1.7 copy.33
  8.3 2.0 copy.32
  10.3 2.7 stack.2
  13.0 7.2 %all-to-all-start = ((bf16[16,64,8,128]{3,2,1,0:T(8,128)(2,1)}), bf16[16,64,8,128]{3,2,1,0:T(8,128)(2,1)}, u32[]{:S(2)}, u32[]{:S(2)}) async-start(bf16[16,64,8,128]{3,2,1,0:T(8,128)(2,1)} %stack.2), calls=%async_computation | async-start | bytes 4194304 | tf_op jit(solution)/shard_map/all_to_all | solution.py:79
  20.6 12.6 %psum.7 = f32[512]{0:T(512)S(1)} all-reduce(f32[512]{0:T(512)S(1)} %fusion.30), channel_id=1, replica_groups=mesh['tok'=16,'head'=8] {'head'}, use_global_device_ids=true, to_apply=%region_4.5 | all-reduce | flops 512 | bytes 4096 | tf_op jit(solution)/shard_map/psum | solution.py:60
  33.3 21.0 %all-to-all-done = bf16[16,64,8,128]{3,2,1,0:T(8,128)(2,1)} async-done(((bf16[16,64,8,128]{3,2,1,0:T(8,128)(2,1)}), bf16[16,64,8,128]{3,2,1,0:T(8,128)(2,1)}, u32[]{:S(2)}, u32[]{:S(2)}) %all-to-all-start) | async-done | bytes 2097184 | tf_op jit(solution)/shard_map/all_to_all | solution.py:79
  54.3 4.1 %copy.34 = bf16[1024,8,128]{0,2,1:T(8,128)(2,1)} copy(bf16[1024,8,128]{2,1,0:T(8,128)(2,1)} %bitcast.15) | data formatting | bytes 4194304 | tf_op jit(solution)/shard_map/reshape | solution.py:78
  58.4 4.2 %fusion.60 = f32[512,1024]{0,1} fusion(bf16[1024,1024]{0,1:T(8,128)(2,1)} %bitcast.128, bf16[512,1024]{1,0:T(8,128)(2,1)S(1)} %copy-done.4, f32[1024]{0:T(1024)S(1)} %convert_element_type.74, f32[512]{0:T(512)S(1)} %add_rsqrt_fusion), kind=kOutput, calls=%fused_computation.106 | convolution fusion | flops 1075838976 | bytes 5249024
  62.6 10.6 %all-gather.5.cloned.1.call-done = bf16[1024,8,128]{2,0,1:T(8,128)(2,1)} async-done(((bf16[64,8,128]{2,0,1:T(8,128)(2,1)}), bf16[1024,8,128]{2,0,1:T(8,128)(2,1)}) %all-gather.5.cloned.1.call-update) | async-done | bytes 2097168 | tf_op jit(solution)/shard_map/all_gather | solution.py:77
  73.2 4.3 %convolution_bitcast_fusion.1 = f32[8,512,128]{1,2,0:T(8,128)} fusion(bf16[1024,8,128]{2,0,1:T(8,128)(2,1)} %all-gather.5.cloned.1.call-done, bf16[512,1024]{1,0:T(8,128)(2,1)S(1)} %copy-done.4, f32[1024]{0:T(1024)S(1)} %convert_element_type.74, f32[512]{0:T(512)S(1)} %add_rsqrt_fusion), kind=kOutput, calls=%fused_computation.48 | convolution fusion | flops 1075838976 | bytes 5249024 | tf_op jit(solution)/shard_map/rd,dnc->nrc/dot_general | solution.py:86
  77.6 67.9 %all-gather.3.cloned.1.call-done = bf16[1024,8,512]{2,0,1:T(8,128)(2,1)} async-done(((bf16[64,8,512]{2,0,1:T(8,128)(2,1)}), bf16[1024,8,512]{2,0,1:T(8,128)(2,1)}) %all-gather.3.cloned.1.call-update) | async-done | bytes 8388624 | tf_op jit(solution)/shard_map/all_gather | solution.py:76
  145.5 7.5 %convolution_bitcast_fusion = f32[8,512,512]{1,2,0:T(8,128)S(1)} fusion(bf16[1024,8,512]{2,0,1:T(8,128)(2,1)} %all-gather.3.cloned.1.call-done, bf16[512,1024]{1,0:T(8,128)(2,1)S(1)} %copy-done.4, f32[1024]{0:T(1024)S(1)} %convert_element_type.74, f32[512]{0:T(512)S(1)} %add_rsqrt_fusion), kind=kOutput, calls=%fused_computation.42 | convolution fusion | flops 4297064448 | bytes 17831936 | tf_op jit(solution)/shard_map/rd,dnc->nrc/dot_general | solution.py:86
  153.0 6.9 %pad_maximum_fusion = f32[8,512,768]{1,2,0:T(8,128)} fusion(f32[8,512,128]{1,2,0:T(8,128)S(1)} %bitcast.125, f32[8,512,128]{1,2,0:T(8,128)S(1)} %copy-done.3, f32[8,512,512]{1,2,0:T(8,128)S(1)} %convolution_bitcast_fusion), kind=kLoop, calls=%fused_computation.41 | loop fusion | flops 6291456 | bytes 25165824 | tf_op jit(solution)/shard_map/concatenate | solution.py:88
  159.9 12.6 %copy.35 = f32[8,512,768]{2,1,0:T(8,128)} copy(f32[8,512,768]{1,2,0:T(8,128)} %pad_maximum_fusion) | data formatting | bytes 25165824 | tf_op jit(solution)/shard_map/concatenate | solution.py:88
  174.7 3.8 scatter_custom_fusion.1
  179.1 5.3 %all-to-all-start.2 = ((bf16[16,1,64]{2,1,0:T(2,128)(2,1)}), bf16[16,1,64]{2,1,0:T(2,128)(2,1)S(1)}, u32[]{:S(2)}, u32[]{:S(2)}) async-start(bf16[16,1,64]{2,1,0:T(2,128)(2,1)} %all_to_all.20), calls=%async_computation.3 | async-start | bytes 16384 | tf_op jit(solution)/shard_map/all_to_all | solution.py:113
  185.2 3.3 gather_fusion.2
  188.5 53.8 %reduce-scatter.2.cloned.1.call-done = f32[512,768]{1,0:T(8,128)} async-done(((f32[4096,768]{1,0:T(8,128)}), f32[512,768]{1,0:T(8,128)}) %reduce-scatter.2.cloned.1.call-update) | async-done | bytes 1572880 | tf_op jit(solution)/shard_map/reduce_scatter | solution.py:89
  242.3 4.6 %scatter_custom_fusion = bf16[1024,768]{1,0:T(8,128)(2,1)} fusion(s32[512]{0:T(512)S(1)} %bitcast.136, f32[512,768]{1,0:T(8,128)} %reduce-scatter.2.cloned.1.call-done, bf16[]{:T(256)} %constant.23.clone.1), kind=kCustom, calls=%fused_computation.62 | custom fusion | flops 393216 | bytes 3145730 | tf_op jit(solution)/shard_map/scatter | solution.py:102
  246.9 7.1 %all-to-all-start.1 = ((bf16[16,64,768]{2,1,0:T(8,128)(2,1)}), bf16[16,64,768]{2,1,0:T(8,128)(2,1)}, u32[]{:S(2)}, u32[]{:S(2)}) async-start(bf16[16,64,768]{2,1,0:T(8,128)(2,1)} %bitcast.20), calls=%async_computation.2 | async-start | bytes 3145728 | tf_op jit(solution)/shard_map/all_to_all | solution.py:106
  254.0 1.5 broadcast_select_fusion
  256.4 1.7 multiply_cosine_fusion.1
  258.1 23.9 %all-to-all-done.1 = bf16[16,64,768]{2,1,0:T(8,128)(2,1)} async-done(((bf16[16,64,768]{2,1,0:T(8,128)(2,1)}), bf16[16,64,768]{2,1,0:T(8,128)(2,1)}, u32[]{:S(2)}, u32[]{:S(2)}) %all-to-all-start.1) | async-done | bytes 1572896 | tf_op jit(solution)/shard_map/all_to_all | solution.py:106
  282.0 1.8 fusion.63
  285.1 3.1 fusion.51
  289.5 1.6 fusion.34
  292.5 1.7 copy.39
  295.4 57.1 %while.10 = (s32[]{:T(128)}, bf16[8,128,4,128]{3,2,1,0:T(4,128)(2,1)}, bf16[8,128,4,128]{3,1,2,0:T(8,128)(2,1)S(1)}, bf16[4096,128]{1,0:T(8,128)(2,1)S(1)}, pred...) while((s32[]{:T(128)}, ...), condition=%wide.region_15.17_spmd, body=%wide.region_10.16_spmd.sunk | while | flops 1365179392 | bytes 36869268 | solution.py:153
  298.1 1.5 fusion.84
  299.6 1.5 fusion.83
  305.2 1.5 fusion.84
  306.7 1.5 fusion.83
  312.3 1.5 fusion.84
  313.9 1.5 fusion.83
  319.5 1.5 fusion.84
  321.0 1.5 fusion.83
  326.6 1.5 fusion.84
  328.1 1.5 fusion.83
  333.7 1.5 fusion.84
  335.2 1.5 fusion.83
  340.9 1.5 fusion.84
  342.4 1.5 fusion.83
  348.0 1.5 fusion.84
  349.5 1.5 fusion.83
  352.4 2.3 reshape.284
  354.7 3.7 all-to-all-start.3
  358.4 18.2 %all-to-all-done.3 = bf16[16,64,512]{2,1,0:T(8,128)(2,1)S(1)} async-done(((bf16[16,64,512]{2,1,0:T(8,128)(2,1)}), bf16[16,64,512]{2,1,0:T(8,128)(2,1)S(1)}, u32[]{:S(2)}, u32[]{:S(2)}) %all-to-all-start.3) | async-done | bytes 1048608 | tf_op jit(solution)/shard_map/all_to_all | solution.py:160
  376.6 2.6 gather_fusion
  (146 shorter events, 42.8 us)
Async XLA Ops:
  6.5 177.9 %copy-start = (bf16[64,128,1,128]{3,1,2,0:T(8,128)(2,1)S(1)}, bf16[64,128,1,128]{3,1,2,0:T(8,128)(2,1)}, u32[]{:S(2)}) copy-start(bf16[64,128,1,128]{3,1,2,0:T(8,128)(2,1)} %param.19) | copy-start | bytes 6291460
  6.5 66.7 %all-gather.5.cloned.1.call-start = ((), (), s32[]{:S(2)}) async-start(), calls=%async_computation.6 | async-start | bytes 2228224 | tf_op jit(solution)/shard_map/all_gather | solution.py:77
  8.3 137.2 %all-gather.3.cloned.1.call-start = ((), (), s32[]{:S(2)}) async-start(), calls=%async_computation.5 | async-start | bytes 8912896 | tf_op jit(solution)/shard_map/all_gather | solution.py:76
  13.0 7.3 %copy-start.7 = (bf16[1024]{0:T(1024)(128)(2,1)S(1)}, bf16[1024]{0:T(1024)(128)(2,1)}, u32[]{:S(2)}) copy-start(bf16[1024]{0:T(1024)(128)(2,1)} %param.14) | copy-start | bytes 6148
  13.0 7.3 %copy-start.4 = (bf16[512,1024]{1,0:T(8,128)(2,1)S(1)}, bf16[512,1024]{1,0:T(8,128)(2,1)}, u32[]{:S(2)}) copy-start(bf16[512,1024]{1,0:T(8,128)(2,1)} %param.13) | copy-start | bytes 3145732
  13.0 41.2 %all-to-all-start = ((bf16[16,64,8,128]{3,2,1,0:T(8,128)(2,1)}), bf16[16,64,8,128]{3,2,1,0:T(8,128)(2,1)}, u32[]{:S(2)}, u32[]{:S(2)}) async-start(bf16[16,64,8,128]{3,2,1,0:T(8,128)(2,1)} %stack.2), calls=%async_computation | async-start | bytes 4194304 | tf_op jit(solution)/shard_map/all_to_all | solution.py:79
  20.2 222.1 %reduce-scatter.2.cloned.1.call-start = ((), (), s32[]{:S(2)}) async-start(), calls=%async_computation.7 | async-start | bytes 14155776 | tf_op jit(solution)/shard_map/reduce_scatter | solution.py:89
  145.5 7.5 %copy-start.2 = (f32[512,1024]{0,1:S(1)}, f32[512,1024]{0,1}, u32[]{:S(2)}) copy-start(f32[512,1024]{0,1} %fusion.60) | copy-start | bytes 6291460
  145.5 7.5 %copy-start.3 = (f32[8,512,128]{1,2,0:T(8,128)S(1)}, f32[8,512,128]{1,2,0:T(8,128)}, u32[]{:S(2)}) copy-start(f32[8,512,128]{1,2,0:T(8,128)} %convolution_bitcast_fusion.1) | copy-start | bytes 6291460
  172.5 0.7 copy-start.6
  172.5 11.9 %copy-start.8 = (s32[1,32]{1,0:T(1,128)S(1)}, s32[1,32]{1,0:T(1,128)}, u32[]{:S(2)}) copy-start(s32[1,32]{1,0:T(1,128)} %param.21) | copy-start | bytes 388
  179.1 67.8 %all-to-all-start.2 = ((bf16[16,1,64]{2,1,0:T(2,128)(2,1)}), bf16[16,1,64]{2,1,0:T(2,128)(2,1)S(1)}, u32[]{:S(2)}, u32[]{:S(2)}) async-start(bf16[16,1,64]{2,1,0:T(2,128)(2,1)} %all_to_all.20), calls=%async_computation.3 | async-start | bytes 16384 | tf_op jit(solution)/shard_map/all_to_all | solution.py:113
  246.9 35.1 %all-to-all-start.1 = ((bf16[16,64,768]{2,1,0:T(8,128)(2,1)}), bf16[16,64,768]{2,1,0:T(8,128)(2,1)}, u32[]{:S(2)}, u32[]{:S(2)}) async-start(bf16[16,64,768]{2,1,0:T(8,128)(2,1)} %bitcast.20), calls=%async_computation.2 | async-start | bytes 3145728 | tf_op jit(solution)/shard_map/all_to_all | solution.py:106
  299.6 1.5 copy-start.5
  306.7 1.5 copy-start.5
  313.9 1.5 copy-start.5
  321.0 1.5 copy-start.5
  328.1 1.5 copy-start.5
  335.2 1.5 copy-start.5
  342.4 1.5 copy-start.5
  349.5 1.5 copy-start.5
  354.7 21.9 %all-to-all-start.3 = ((bf16[16,64,512]{2,1,0:T(8,128)(2,1)}), bf16[16,64,512]{2,1,0:T(8,128)(2,1)S(1)}, u32[]{:S(2)}, u32[]{:S(2)}) async-start(bf16[16,64,512]{2,1,0:T(8,128)(2,1)} %reshape.284), calls=%async_computation.4 | async-start | bytes 2097152 | tf_op jit(solution)/shard_map/all_to_all | solution.py:160
  376.6 2.6 copy-start.1
Sparse Core Ops, SparseCore 0:
  9.5 63.7 all-gather.4
  75.4 70.0 all-gather.2
  172.6 69.6 reduce-scatter.1
